TPU v7x, 512 devices: a whole 4x4x16 slice. The times are simulated.
512 devices in a mesh: ax: 32 (over z, x_hi), pen: 16 (over x_lo, y, core).
Axes of the slice: x: 4 (x_hi: 2, x_lo: 2; x = x_hi * 2 + x_lo), y: 4, z: 16, core: 2. Of those that a mesh axis runs over, the one named last changes fastest.
Arguments:
- fields: float32 [2, 5, 512, 192, 128], P(None, None, 'ax', 'pen'), may hold values from -0.8 to 0.8, as said below
- axial_mean: float32 [512, 192, 128], P('ax', 'pen'), may hold values from 0.2 to 1.5
- radial_mean: float32 [512, 192, 128], P('ax', 'pen'), may hold values from -0.3 to 0.3
- swirl_mean: float32 [512, 192, 128], P('ax', 'pen'), may hold values from -0.3 to 0.3
- density: float32 [512, 192, 128], P('ax', 'pen'), may hold values from 0.5 to 2
- pressure: float32 [512, 192, 128], P('ax', 'pen'), may hold values from 0.4 to 1.2
Outputs:
- residual: float32 [2, 5, 512, 192, 128], P(None, None, 'ax', 'pen')
Inputs may be any that keep to these rules, and one draw needn't show every extreme that they name: `fields`: each entry is a draw times (1 - c_j^2)^2 with c_j = cos(pi j / 191) at radial node j, so every field vanishes at both radial ends.
All inputs are finite; a program needn't handle non-finite values.
Results may differ from a plain program's by a relative error of at most 0.0001.
Values sent between devices are 32-bit elements; how exact they have to be, the bound alone decides.
No kernel may reach another device: no remote copies, remote signals or barrier semaphores. Data moves between devices by JAX's collectives and lax.ppermute only.
A program may use at most 64 MiB of HBM per device.

v0:
```python
import jax
import jax.numpy as jnp
import numpy as np
from jax import lax
from jax.sharding import PartitionSpec as P

angular_frequency = 1.7
viscosity = 0.01
conduction = 0.014
gamma_ratio = 1.4
spacing = 0.1
radius_inner = 0.5
radius_outer = 6.5
first_axial = (0.8, -0.2, 4.0 / 105.0, -1.0 / 280.0)
axial_second_derivative = (-205.0 / 72.0, 1.6, -0.2, 8.0 / 315.0, -1.0 / 560.0)
highest = lax.Precision.HIGHEST


def with_halo(array, sides, width):
    for axis, dim in sides:
        size, length = (lax.axis_size(axis), array.shape[dim])
        up = [(i, (i + 1) % size) for i in range(size - 1)]
        down = [(j, i) for i, j in up]
        last = lax.slice_in_dim(array, length - width, length, axis=dim)
        initial = lax.slice_in_dim(array, 0, width, axis=dim)
        before = lax.ppermute(last, axis, up)
        after = lax.ppermute(initial, axis, down)
        array = jnp.concatenate([before, array, after], axis=dim)
    return array


def cheb_tables(node_count):
    last_node = node_count - 1
    node_index = np.arange(node_count)
    cheb_nodes = np.cos(np.pi * node_index / last_node)
    end_weight = np.where((node_index == 0) | (node_index == last_node), 2.0, 1.0) * np.where(
        node_index % 2 == 0, 1.0, -1.0
    )
    row_index = node_index[:, None]
    col_index = node_index[None, :]
    node_gap = (
        -2.0
        * np.sin(np.pi * (row_index + col_index) / (2 * last_node))
        * np.sin(np.pi * (row_index - col_index) / (2 * last_node))
    )
    off_diag = row_index != col_index
    safe_gap = np.where(off_diag, node_gap, 1.0)
    matrix = np.where(off_diag, end_weight[:, None] / end_weight[None, :] / safe_gap, 0.0)
    row_total = matrix.sum(axis=1)
    matrix = np.where(off_diag, matrix, -row_total[:, None])
    order_first_terms = matrix * (-2.0 / (radius_outer - radius_inner))
    second_order = order_first_terms @ order_first_terms
    radius_nodes = radius_inner + (radius_outer - radius_inner) * (1.0 - cheb_nodes) / 2.0
    return (order_first_terms, second_order, radius_nodes)


def fourier_tables(point_count):
    offsets = np.arange(point_count)[:, None] - np.arange(point_count)[None, :]
    half_angle = np.pi * offsets / point_count
    sign_table = np.where(offsets % 2 == 0, 1.0, -1.0)
    nonzero = offsets != 0
    safe_sine = np.where(nonzero, np.sin(half_angle), 1.0)
    order_first_terms = np.where(nonzero, 0.5 * sign_table * np.cos(half_angle) / safe_sine, 0.0)
    second_order = np.where(
        nonzero, -0.5 * sign_table / safe_sine**2, -(point_count**2) / 12.0 - 1.0 / 6.0
    )
    return (order_first_terms, second_order)


def build_work(fields, density, pressure):
    thermal_field = fields[:, 4] / density - pressure * fields[:, 3] / (density * density)
    return jnp.concatenate([fields[:, :3], thermal_field[:, None], fields[:, 3:]], axis=1)


def axial_derivatives(padded, planes):

    def shifted(source, offset):
        return lax.slice_in_dim(source, 4 + offset, 4 + offset + planes, axis=2)

    lower = padded[:, :4]
    slope_x = first_axial[0] * (shifted(padded, 1) - shifted(padded, -1))
    curve_x = axial_second_derivative[0] * shifted(lower, 0)
    for offset in range(1, 5):
        if offset > 1:
            slope_x = slope_x + first_axial[offset - 1] * (
                shifted(padded, offset) - shifted(padded, -offset)
            )
        curve_x = curve_x + axial_second_derivative[offset] * (
            shifted(lower, offset) + shifted(lower, -offset)
        )
    return (slope_x / spacing, curve_x / (spacing * spacing))


def theta_derivatives(work_fields, theta_first, azimuthal_second_derivative):
    slope_t = jnp.dot(work_fields, theta_first, precision=highest)
    curve_t = jnp.dot(work_fields[:, :4], azimuthal_second_derivative, precision=highest)
    return (slope_t, curve_t)


def radial_derivatives(pencil_block, radial_first, radial_second):
    slope_r = jnp.einsum("sj,abxjt->abxst", radial_first, pencil_block, precision=highest)
    curve_r = jnp.einsum("sj,abxjt->abxst", radial_second, pencil_block[:, :4], precision=highest)
    return (slope_r, curve_r)


def rotate_phase(value):
    return jnp.stack([-angular_frequency * value[1], angular_frequency * value[0]])


def radial_terms(slope_r, curve_r, radial_mean, density, pressure, inv_radius):
    laplace = curve_r + slope_r[:, :4] * inv_radius
    convect = radial_mean * slope_r
    term_u = convect[:, 0] - viscosity * laplace[:, 0]
    term_v = convect[:, 1] + slope_r[:, 5] / density - viscosity * laplace[:, 1]
    term_w = convect[:, 2] - viscosity * laplace[:, 2]
    term_rho = convect[:, 4] + density * slope_r[:, 1]
    term_p = convect[:, 5] + gamma_ratio * pressure * slope_r[:, 1] - conduction * laplace[:, 3]
    return jnp.stack([term_u, term_v, term_w, term_rho, term_p], axis=1)


def other_terms(
    work_fields,
    slope_x,
    curve_x,
    slope_t,
    curve_t,
    axial_mean,
    radial_mean,
    swirl_mean,
    density,
    pressure,
    inv_radius,
):
    inv_square = inv_radius * inv_radius
    convect = axial_mean * slope_x + swirl_mean * inv_radius * slope_t
    laplace = curve_x + inv_square * curve_t
    vel_u = work_fields[:, 0]
    vel_v = work_fields[:, 1]
    vel_w = work_fields[:, 2]
    div_part = slope_x[:, 0] + inv_radius * (vel_v + slope_t[:, 2])
    term_u = (
        rotate_phase(vel_u) + convect[:, 0] + slope_x[:, 5] / density - viscosity * laplace[:, 0]
    )
    term_v = (
        rotate_phase(vel_v)
        + convect[:, 1]
        - 2.0 * swirl_mean * inv_radius * vel_w
        - viscosity * (laplace[:, 1] - inv_square * (vel_v + 2.0 * slope_t[:, 2]))
    )
    term_w = (
        rotate_phase(vel_w)
        + convect[:, 2]
        + inv_radius * slope_t[:, 5] / density
        + inv_radius * (radial_mean * vel_w + swirl_mean * vel_v)
        - viscosity * (laplace[:, 2] - inv_square * (vel_w - 2.0 * slope_t[:, 1]))
    )
    term_rho = rotate_phase(work_fields[:, 4]) + convect[:, 4] + density * div_part
    term_p = (
        rotate_phase(work_fields[:, 5])
        + convect[:, 5]
        + gamma_ratio * pressure * div_part
        - conduction * laplace[:, 3]
    )
    return jnp.stack([term_u, term_v, term_w, term_rho, term_p], axis=1)


def per_device(fields, axial_mean, radial_mean, swirl_mean, density, pressure):
    planes = fields.shape[2]
    shard_rows = fields.shape[3]
    grid_points = fields.shape[4]
    total_rows = shard_rows * lax.axis_size("pen")
    first_np, second_np, radius_np = cheb_tables(total_rows)
    radial_first = jnp.asarray(first_np, jnp.float32)
    radial_second = jnp.asarray(second_np, jnp.float32)
    inv_all = jnp.asarray(1.0 / radius_np, jnp.float32)[:, None]
    inv_local = lax.dynamic_slice_in_dim(inv_all, lax.axis_index("pen") * shard_rows, shard_rows, 0)
    theta_np, theta_second_np = fourier_tables(grid_points)
    theta_first = jnp.asarray(theta_np.T, jnp.float32)
    azimuthal_second_derivative = jnp.asarray(theta_second_np.T, jnp.float32)
    work_fields = build_work(fields, density, pressure)
    padded = with_halo(work_fields, (("ax", 2),), 4)
    slope_x, curve_x = axial_derivatives(padded, planes)
    slope_t, curve_t = theta_derivatives(work_fields, theta_first, azimuthal_second_derivative)
    slope_r, curve_r = radial_derivatives(
        lax.all_to_all(work_fields, "pen", split_axis=2, concat_axis=3, tiled=True),
        radial_first,
        radial_second,
    )
    slope_r, curve_r = (
        lax.all_to_all(slope_r, "pen", split_axis=3, concat_axis=2, tiled=True),
        lax.all_to_all(curve_r, "pen", split_axis=3, concat_axis=2, tiled=True),
    )
    radial_component = radial_terms(slope_r, curve_r, radial_mean, density, pressure, inv_local)
    return radial_component + other_terms(
        work_fields,
        slope_x,
        curve_x,
        slope_t,
        curve_t,
        axial_mean,
        radial_mean,
        swirl_mean,
        density,
        pressure,
        inv_local,
    )


def solution(mesh):
    placed = (
        P(None, None, "ax", "pen", None),
        P("ax", "pen", None),
        P("ax", "pen", None),
        P("ax", "pen", None),
        P("ax", "pen", None),
        P("ax", "pen", None),
    )
    return jax.shard_map(
        per_device,
        mesh=mesh,
        in_specs=placed,
        out_specs=P(None, None, "ax", "pen", None),
        check_vma=False,
    )
```

profile of v0, /device:TPU:4, one launch (start us, length us, event | category | flops | bytes accessed | tf_op | source)
XLA Modules:
  0.0 97.6 jit_solution(14125094061628838863)
XLA Ops:
  0.0 1.2 %slice.244 = f32[2,3,16,12,128]{4,2,3,1,0:T(8,128)S(1)} slice(f32[2,5,16,12,128]{4,2,3,1,0:T(8,128)} %param.11), slice={[0:2], [0:3], [0:16], [0:12], [0:128]} | slice | bytes 1179648 | tf_op jit(solution)/shard_map/slice | solution.py:72
  1.2 0.2 copy-done
  1.5 0.1 divide_subtract_fusion
  1.5 0.1 pad_maximum_fusion.1
  1.6 2.0 %copy.44 = f32[2,6,16,12,128]{4,0,3,1,2:T(2,128)} copy(f32[2,6,16,12,128]{4,2,3,1,0:T(8,128)S(1)} %pad_maximum_fusion.1) | data formatting | bytes 2359296 | tf_op jit(solution)/shard_map/concatenate | solution.py:72
  3.6 5.3 %all-to-all-start = ((f32[2,6,16,12,128]{4,0,3,1,2:T(2,128)}), f32[2,6,16,12,128]{4,0,3,1,2:T(2,128)}, u32[]{:S(2)}, u32[]{:S(2)}) async-start(f32[2,6,16,12,128]{4,0,3,1,2:T(2,128)} %copy.44), calls=%async_computation | async-start | bytes 2359296 | tf_op jit(solution)/shard_map/all_to_all | solution.py:185
  8.8 0.0 copy-start.25
  8.8 0.0 copy-start.8
  8.9 0.9 fusion.53
  9.8 6.9 %collective-permute-start = (f32[2,6,4,12,128]{4,2,3,1,0:T(4,128)}, f32[2,6,4,12,128]{4,2,3,1,0:T(4,128)S(1)}, u32[]{:S(2)}, u32[]{:S(2)}) collective-permute-start(f32[2,6,4,12,128]{4,2,3,1,0:T(4,128)} %get-tuple-element.11), channel_id=1, source_target_pairs={{16,0},{32,16},{48,32},{64,48},{80,64},{96,80},{112,96},{128,112},... | collective-permute-start | bytes 884744 | tf_op jit(solution)/shard_map/ppermute | solution.py:27
  16.7 1.9 %collective-permute-start.1 = (f32[2,6,4,12,128]{4,2,3,1,0:T(4,128)}, f32[2,6,4,12,128]{4,2,3,1,0:T(4,128)S(1)}, u32[]{:S(2)}, u32[]{:S(2)}) collective-permute-start(f32[2,6,4,12,128]{4,2,3,1,0:T(4,128)} %get-tuple-element.12), channel_id=1, source_target_pairs={{0,16},{16,32},{32,48},{48,64},{64,80},{80,96},{96,112},{112,128},... | collective-permute-start | bytes 884744 | tf_op jit(solution)/shard_map/ppermute | solution.py:26
  18.6 0.1 broadcast_multiply_fusion.6
  18.7 1.7 %broadcast_multiply_fusion.2 = (f32[16,12,128]{2,0,1:T(8,128)}, f32[16,12,128]{2,0,1:T(8,128)}, f32[16,12,128]{2,0,1:T(8,128)}) fusion(f32[16,12,128]{2,0,1:T(8,128)S(1)} %copy-done.8, f32[12]{0:T(128)S(1)} %get-tuple-element.30, f32[12]{0:T(128)S(1)} %get-tuple-element.32, f32[16,12,128]{2,0,1:T(8,128)} %param.12), kind=kLoop, calls=%fused_computation.100 | loop fusion | flops 73728 | bytes 491616 | tf_op jit(solution)/shard_map/mul | solution.py:147
  20.4 0.9 broadcast_multiply_fusion.5
  21.3 1.0 slice_multiply_fusion.10
  22.3 6.7 %collective-permute-done = f32[2,6,4,12,128]{4,2,3,1,0:T(4,128)S(1)} collective-permute-done((f32[2,6,4,12,128]{4,2,3,1,0:T(4,128)}, f32[2,6,4,12,128]{4,2,3,1,0:T(4,128)S(1)}, u32[]{:S(2)}, u32[]{:S(2)}) %collective-permute-start) | collective-permute-done | bytes 294944 | tf_op jit(solution)/shard_map/ppermute | solution.py:27
  28.9 11.4 %collective-permute-done.1 = f32[2,6,4,12,128]{4,2,3,1,0:T(4,128)S(1)} collective-permute-done((f32[2,6,4,12,128]{4,2,3,1,0:T(4,128)}, f32[2,6,4,12,128]{4,2,3,1,0:T(4,128)S(1)}, u32[]{:S(2)}, u32[]{:S(2)}) %collective-permute-start.1) | collective-permute-done | bytes 294944 | tf_op jit(solution)/shard_map/ppermute | solution.py:26
  40.4 2.1 %pad_maximum_fusion = (f32[2,6,20,12,128]{4,2,3,1,0:T(8,128)}, f32[2,6,20,12,128]{4,2,3,1,0:T(8,128)}) fusion(f32[2,6,4,12,128]{4,2,3,1,0:T(4,128)S(1)} %collective-permute-done, f32[2,2,16,12,128]{4,2,3,1,0:T(8,128)S(1)} %slice.247, f32[2,1,16,12,128]{4,2,3,1,0:T(8,128)S(1)} %divide_subtract_fusion, f32[2,3,16,12,128]{4,2,3,1,0:T(8,128)S(1)} %slice.244, ...), kind=kLoop, calls=%fused_computation | loop fusion | flops 2211840 | bytes 4718592 | tf_op jit(solution)/shard_map/concatenate | solution.py:28
  42.5 1.4 %copy.45 = f32[2,6,16,12,128]{4,0,3,2,1:T(2,128)S(1)} copy(f32[2,6,16,12,128]{4,0,3,1,2:T(2,128)} %all-to-all-done) | data formatting | bytes 2359296 | tf_op jit(solution)/shard_map/all_to_all | solution.py:185
  43.9 1.2 %convolution_bitcast_fusion = f32[2,6,1,192,128]{4,3,1,0,2:T(8,128)S(1)} fusion(f32[192,192,1,1]{1,0,3,2:T(8,128)S(1)} %copy-done.24, f32[2,6,192,128]{3,0,2,1:T(2,128)S(1)} %bitcast.35), kind=kOutput, calls=%fused_computation.2 | convolution fusion | flops 679477248 | bytes 2506752 | tf_op jit(solution)/shard_map/sj,abxjt->abxst/dot_general | solution.py:101
  45.1 1.9 %copy.47 = f32[2,6,1,192,128]{4,0,2,1,3:T(2,128)} copy(f32[2,6,1,192,128]{4,3,1,0,2:T(8,128)S(1)} %convolution_bitcast_fusion) | data formatting | bytes 2359296 | tf_op jit(solution)/shard_map/sj,abxjt->abxst/transpose | solution.py:101
  47.1 6.2 %all-to-all-start.1 = ((f32[2,6,1,192,128]{4,0,2,1,3:T(2,128)}), f32[2,6,1,192,128]{4,0,2,1,3:T(2,128)}, u32[]{:S(2)}, u32[]{:S(2)}) async-start(f32[2,6,1,192,128]{4,0,2,1,3:T(2,128)} %copy.47), calls=%async_computation.1 | async-start | bytes 2359296 | tf_op jit(solution)/shard_map/all_to_all | solution.py:190
  53.3 8.7 %multiply_add_fusion = (f32[2,6,16,12,128]{4,2,3,1,0:T(8,128)S(1)}, f32[2,6,16,12,128]{4,2,3,1,0:T(8,128)S(1)}, f32[2,6,16,12,128]{4,2,3,1,0:T(8,128)}) fusion(f32[16,12,128]{2,0,1:T(8,128)} %get-tuple-element.29, f32[16,12,128]{2,0,1:T(8,128)} %get-tuple-element.34, f32[2,6,20,12,128]{4,2,3,1,0:T(8,128)} %get-tuple-element.10, ...), kind=kOutput, calls=%fused_computation.19 | convolution fusion | flops 457703424 | bytes 14417920 | tf_op jit(solution)/shard_map/dot_general | solution.py:95
  62.0 0.1 broadcast_multiply_fusion
  62.1 0.8 copy-done.26
  62.9 5.3 %fusion = f32[2,4,16,12,128]{4,2,3,1,0:T(8,128)S(1)} fusion(f32[128,128,1,1,1]{1,0,4,3,2:T(8,128)S(1)} %copy-done.26, f32[2,6,20,12,128]{4,2,3,1,0:T(8,128)} %get-tuple-element.10, f32[2,6,20,12,128]{4,2,3,1,0:T(8,128)} %get-tuple-element.9, f32[2,1,16,12,128]{4,2,3,1,0:T(8,128)S(1)} %divide_subtract_fusion, f32[2,3,16,12,128]{4,2,3,1,0:T(8,128)S(1)} %slice.244, ...), kind=kOutput, calls=%fused_computation.5 | convolution fusion | flops 305528832 | bytes 8716800 | tf_op jit(solution)/shard_map/dot_general | solution.py:96
  68.3 0.0 copy-start.23
  68.3 0.1 fusion.38
  68.4 0.1 slice.306
  68.4 0.7 copy-done.6
  69.1 0.3 copy-done.23
  69.4 0.9 convolution_bitcast_fusion.1
  70.3 1.4 %copy.52 = f32[2,4,1,192,128]{4,1,0,2,3:T(4,128)} copy(f32[2,4,1,192,128]{4,3,1,0,2:T(8,128)S(1)} %convolution_bitcast_fusion.1) | data formatting | bytes 1572864 | tf_op jit(solution)/shard_map/sj,abxjt->abxst/transpose | solution.py:102
  71.7 0.0 copy-start.10
  71.7 5.9 %all-to-all-start.2 = ((f32[2,4,1,192,128]{4,1,0,2,3:T(4,128)}), f32[2,4,1,192,128]{4,1,0,2,3:T(4,128)}, u32[]{:S(2)}, u32[]{:S(2)}) async-start(f32[2,4,1,192,128]{4,1,0,2,3:T(4,128)} %copy.52), calls=%async_computation.2 | async-start | bytes 1572864 | tf_op jit(solution)/shard_map/all_to_all | solution.py:191
  77.6 1.2 %fusion.35 = f32[2,5,16,12,128]{4,2,3,1,0:T(8,128)S(1)} fusion(f32[2,5,16,12,128]{4,2,3,1,0:T(8,128)S(1)} %fusion.38, f32[2,4,16,12,128]{4,2,3,1,0:T(8,128)S(1)} %copy-done.7, f32[2,6,16,12,128]{4,2,3,1,0:T(8,128)} %copy-done.5, f32[1,1,16,12,128]{4,2,3,1,0:T(8,128)S(1)} %copy-done.22, f32[1,1,16,12,128]{4,2,3,1,0:T(8,128)} %get-tuple-element.20, ...), kind=kLoop, calls=%fused_computation.63 | loop fusion | flops 491520 | bytes 1475072
  78.8 0.0 copy-start.11
  78.9 1.3 %fusion.29 = f32[2,5,16,12,128]{4,2,3,1,0:T(8,128)S(1)} fusion(f32[2,5,16,12,128]{4,2,3,1,0:T(8,128)S(1)} %fusion.35, f32[2,6,16,12,128]{4,2,3,1,0:T(8,128)} %get-tuple-element.33, f32[2,4,16,12,128]{4,2,3,1,0:T(8,128)S(1)} %copy-done.7, f32[2,6,16,12,128]{4,2,3,1,0:T(8,128)} %copy-done.5, f32[1,1,16,12,128]{4,2,3,1,0:T(8,128)S(1)} %copy-done.16, ...), kind=kLoop, calls=%fused_computation.54 | loop fusion | flops 786432 | bytes 1868800
  80.1 0.0 copy-start.3
  80.1 0.9 copy-done.3
  81.1 1.7 %broadcast_multiply_fusion.1 = (f32[2,6,16,12,128]{4,2,3,1,0:T(8,128)S(1)}, f32[2,6,16,12,128]{4,2,3,1,0:T(8,128)S(1)}) fusion(f32[16,12,128]{2,0,1:T(8,128)S(1)} %copy-done.11, f32[2,6,16,12,128]{4,0,1,3,2:T(2,128)} %bitcast.6), kind=kLoop, calls=%fused_computation.38 | loop fusion | flops 294912 | bytes 3637248 | tf_op jit(solution)/shard_map/mul | solution.py:112
  82.7 8.6 %all-to-all-done.2 = f32[2,4,1,192,128]{4,1,0,2,3:T(4,128)} async-done(((f32[2,4,1,192,128]{4,1,0,2,3:T(4,128)}), f32[2,4,1,192,128]{4,1,0,2,3:T(4,128)}, u32[]{:S(2)}, u32[]{:S(2)}) %all-to-all-start.2) | async-done | bytes 786464 | tf_op jit(solution)/shard_map/all_to_all | solution.py:191
  91.4 1.7 %fusion.18 = f32[2,4,16,12,128]{4,2,3,1,0:T(8,128)S(1)} fusion(f32[2,6,16,12,128]{4,2,3,1,0:T(8,128)S(1)} %get-tuple-element.14, f32[2,4,16,12,128]{4,1,0,3,2:T(4,128)} %bitcast.13, f32[12]{0:T(128)S(1)} %get-tuple-element.32), kind=kLoop, calls=%fused_computation.34 | loop fusion | flops 393216 | bytes 2359344 | tf_op jit(solution)/shard_map/add | solution.py:111
  93.2 1.2 %fusion.23 = (f32[2,5,16,12,128]{4,2,3,1,0:T(8,128)S(1)}, f32[2,1,16,12,128]{4,2,3,1,0:T(8,128)S(1)}, f32[2,5,16,12,128]{4,2,3,1,0:T(8,128)S(1)}) fusion(f32[2,5,16,12,128]{4,2,3,1,0:T(8,128)S(1)} %copy-done.4, f32[2,6,16,12,128]{4,2,3,1,0:T(8,128)} %copy-done.5, f32[1,1,16,12,128]{4,2,3,1,0:T(8,128)S(1)} %copy-done.15, ...), kind=kLoop, calls=%fused_computation.47 | loop fusion | flops 540672 | bytes 2261504
  94.5 0.8 copy-done.12
  95.3 0.0 copy-done.13
  95.3 1.1 %fusion.20 = (f32[2,5,16,12,128]{4,2,3,1,0:T(8,128)S(1)}, f32[2,5,16,12,128]{4,2,3,1,0:T(8,128)S(1)}) fusion(f32[2,5,16,12,128]{4,2,3,1,0:T(8,128)S(1)} %get-tuple-element.5, f32[2,4,16,12,128]{4,2,3,1,0:T(8,128)} %copy-done.6, f32[2,6,16,12,128]{4,2,3,1,0:T(8,128)} %copy-done.5, f32[1,1,16,12,128]{4,2,3,1,0:T(8,128)S(1)} %copy-done.13, ...), kind=kLoop, calls=%fused_computation.41 | loop fusion | flops 491520 | bytes 1867776 | tf_op jit(solution)/shard_map/stack | solution.py:164
  96.5 1.1 %add.150 = f32[2,5,16,12,128]{4,2,3,1,0:T(8,128)} add(f32[2,5,16,12,128]{4,2,3,1,0:T(8,128)S(1)} %get-tuple-element.26, f32[2,5,16,12,128]{4,2,3,1,0:T(8,128)S(1)} %get-tuple-element.25) | non-fusion elementwise | flops 245760 | bytes 2949120 | tf_op jit(solution)/shard_map/add | solution.py:194
  (48 shorter events, 0.2 us)
Async XLA Ops:
  0.0 1.4 %copy-start = (f32[2,5,16,12,128]{4,2,3,1,0:T(8,128)S(1)}, f32[2,5,16,12,128]{4,2,3,1,0:T(8,128)}, u32[]{:S(2)}) copy-start(f32[2,5,16,12,128]{4,2,3,1,0:T(8,128)} %param.11) | copy-start | bytes 2949124
  0.0 1.4 %copy-start.1 = (f32[16,12,128]{2,0,1:T(8,128)S(1)}, f32[16,12,128]{2,0,1:T(8,128)}, u32[]{:S(2)}) copy-start(f32[16,12,128]{2,0,1:T(8,128)} %param.15) | copy-start | bytes 294916
  0.0 1.4 %copy-start.18 = (f32[16,12,128]{2,0,1:T(8,128)S(1)}, f32[16,12,128]{2,0,1:T(8,128)}, u32[]{:S(2)}) copy-start(f32[16,12,128]{2,0,1:T(8,128)} %param.16) | copy-start | bytes 294916
  3.6 38.9 %all-to-all-start = ((f32[2,6,16,12,128]{4,0,3,1,2:T(2,128)}), f32[2,6,16,12,128]{4,0,3,1,2:T(2,128)}, u32[]{:S(2)}, u32[]{:S(2)}) async-start(f32[2,6,16,12,128]{4,0,3,1,2:T(2,128)} %copy.44), calls=%async_computation | async-start | bytes 2359296 | tf_op jit(solution)/shard_map/all_to_all | solution.py:185
  8.8 9.8 %copy-start.25 = (f32[192]{0:T(256)S(1)}, f32[192]{0:T(256)}, u32[]{:S(2)}) copy-start(f32[192]{0:T(256)} %constant.58.clone) | copy-start | bytes 2308
  8.8 9.8 %copy-start.8 = (f32[16,12,128]{2,0,1:T(8,128)S(1)}, f32[16,12,128]{2,0,1:T(8,128)}, u32[]{:S(2)}) copy-start(f32[16,12,128]{2,0,1:T(8,128)} %param.14) | copy-start | bytes 294916
  9.8 19.2 %collective-permute-start = (f32[2,6,4,12,128]{4,2,3,1,0:T(4,128)}, f32[2,6,4,12,128]{4,2,3,1,0:T(4,128)S(1)}, u32[]{:S(2)}, u32[]{:S(2)}) collective-permute-start(f32[2,6,4,12,128]{4,2,3,1,0:T(4,128)} %get-tuple-element.11), channel_id=1, source_target_pairs={{16,0},{32,16},{48,32},{64,48},{80,64},{96,80},{112,96},{128,112},... | collective-permute-start | bytes 884744 | tf_op jit(solution)/shard_map/ppermute | solution.py:27
  16.7 23.7 %collective-permute-start.1 = (f32[2,6,4,12,128]{4,2,3,1,0:T(4,128)}, f32[2,6,4,12,128]{4,2,3,1,0:T(4,128)S(1)}, u32[]{:S(2)}, u32[]{:S(2)}) collective-permute-start(f32[2,6,4,12,128]{4,2,3,1,0:T(4,128)} %get-tuple-element.12), channel_id=1, source_target_pairs={{0,16},{16,32},{32,48},{48,64},{64,80},{80,96},{96,112},{112,128},... | collective-permute-start | bytes 884744 | tf_op jit(solution)/shard_map/ppermute | solution.py:26
  42.5 1.4 %copy-start.24 = (f32[192,192,1,1]{1,0,3,2:T(8,128)S(1)}, f32[192,192,1,1]{1,0,3,2:T(8,128)}, u32[]{:S(2)}) copy-start(f32[192,192,1,1]{1,0,3,2:T(8,128)} %constant.67) | copy-start | bytes 442372
  47.1 24.6 %all-to-all-start.1 = ((f32[2,6,1,192,128]{4,0,2,1,3:T(2,128)}), f32[2,6,1,192,128]{4,0,2,1,3:T(2,128)}, u32[]{:S(2)}, u32[]{:S(2)}) async-start(f32[2,6,1,192,128]{4,0,2,1,3:T(2,128)} %copy.47), calls=%async_computation.1 | async-start | bytes 2359296 | tf_op jit(solution)/shard_map/all_to_all | solution.py:190
  62.0 6.2 %copy-start.5 = (f32[2,6,16,12,128]{4,2,3,1,0:T(8,128)}, f32[2,6,16,12,128]{4,2,3,1,0:T(8,128)S(1)}, u32[]{:S(2)}) copy-start(f32[2,6,16,12,128]{4,2,3,1,0:T(8,128)S(1)} %get-tuple-element.7) | copy-start | bytes 3538948
  62.0 0.9 copy-start.26
  62.1 6.1 %copy-start.2 = (f32[2,6,16,12,128]{4,2,3,1,0:T(8,128)}, f32[2,6,16,12,128]{4,2,3,1,0:T(8,128)S(1)}, u32[]{:S(2)}) copy-start(f32[2,6,16,12,128]{4,2,3,1,0:T(8,128)S(1)} %broadcast_multiply_fusion) | copy-start | bytes 3538948
  62.9 5.4 %copy-start.19 = (f32[1,1,16,12,128]{4,2,3,1,0:T(8,128)S(1)}, f32[1,1,16,12,128]{4,2,3,1,0:T(8,128)}, u32[]{:S(2)}) copy-start(f32[1,1,16,12,128]{4,2,3,1,0:T(8,128)} %get-tuple-element.21) | copy-start | bytes 294916
  62.9 5.4 %copy-start.20 = (f32[1,1,16,12,128]{4,2,3,1,0:T(8,128)S(1)}, f32[1,1,16,12,128]{4,2,3,1,0:T(8,128)}, u32[]{:S(2)}) copy-start(f32[1,1,16,12,128]{4,2,3,1,0:T(8,128)} %get-tuple-element.22) | copy-start | bytes 294916
  68.2 0.9 copy-start.6
  68.3 1.2 %copy-start.23 = (f32[192,192,1,1]{1,0,3,2:T(8,128)S(1)}, f32[192,192,1,1]{1,0,3,2:T(8,128)}, u32[]{:S(2)}) copy-start(f32[192,192,1,1]{1,0,3,2:T(8,128)} %constant.68) | copy-start | bytes 442372
  71.7 5.9 %copy-start.7 = (f32[2,4,16,12,128]{4,2,3,1,0:T(8,128)S(1)}, f32[2,4,16,12,128]{4,2,3,1,0:T(8,128)}, u32[]{:S(2)}) copy-start(f32[2,4,16,12,128]{4,2,3,1,0:T(8,128)} %copy-done.6) | copy-start | bytes 2359300
  71.7 5.9 %copy-start.21 = (f32[16,12,128]{2,0,1:T(8,128)S(1)}, f32[16,12,128]{2,0,1:T(8,128)}, u32[]{:S(2)}) copy-start(f32[16,12,128]{2,0,1:T(8,128)} %get-tuple-element.28) | copy-start | bytes 294916
  71.7 5.9 %copy-start.22 = (f32[1,1,16,12,128]{4,2,3,1,0:T(8,128)S(1)}, f32[1,1,16,12,128]{4,2,3,1,0:T(8,128)}, u32[]{:S(2)}) copy-start(f32[1,1,16,12,128]{4,2,3,1,0:T(8,128)} %get-tuple-element.19) | copy-start | bytes 294916
  71.7 7.1 %copy-start.9 = (f32[16,12,128]{2,0,1:T(8,128)S(1)}, f32[16,12,128]{2,0,1:T(8,128)}, u32[]{:S(2)}) copy-start(f32[16,12,128]{2,0,1:T(8,128)} %param.14) | copy-start | bytes 294916
  71.7 7.1 %copy-start.10 = (f32[16,12,128]{2,0,1:T(8,128)S(1)}, f32[16,12,128]{2,0,1:T(8,128)}, u32[]{:S(2)}) copy-start(f32[16,12,128]{2,0,1:T(8,128)} %param.13) | copy-start | bytes 294916
  71.7 7.1 %copy-start.16 = (f32[1,1,16,12,128]{4,2,3,1,0:T(8,128)S(1)}, f32[1,1,16,12,128]{4,2,3,1,0:T(8,128)}, u32[]{:S(2)}) copy-start(f32[1,1,16,12,128]{4,2,3,1,0:T(8,128)} %get-tuple-element.17) | copy-start | bytes 294916
  71.7 7.1 %copy-start.17 = (f32[1,1,16,12,128]{4,2,3,1,0:T(8,128)S(1)}, f32[1,1,16,12,128]{4,2,3,1,0:T(8,128)}, u32[]{:S(2)}) copy-start(f32[1,1,16,12,128]{4,2,3,1,0:T(8,128)} %get-tuple-element.18) | copy-start | bytes 294916
  71.7 19.6 %all-to-all-start.2 = ((f32[2,4,1,192,128]{4,1,0,2,3:T(4,128)}), f32[2,4,1,192,128]{4,1,0,2,3:T(4,128)}, u32[]{:S(2)}, u32[]{:S(2)}) async-start(f32[2,4,1,192,128]{4,1,0,2,3:T(4,128)} %copy.52), calls=%async_computation.2 | async-start | bytes 1572864 | tf_op jit(solution)/shard_map/all_to_all | solution.py:191
  78.8 2.3 %copy-start.11 = (f32[16,12,128]{2,0,1:T(8,128)S(1)}, f32[16,12,128]{2,0,1:T(8,128)}, u32[]{:S(2)}) copy-start(f32[16,12,128]{2,0,1:T(8,128)} %param.13) | copy-start | bytes 294916
  80.1 0.9 copy-start.3
  91.4 1.8 %copy-start.4 = (f32[2,5,16,12,128]{4,2,3,1,0:T(8,128)S(1)}, f32[2,5,16,12,128]{4,2,3,1,0:T(8,128)}, u32[]{:S(2)}) copy-start(f32[2,5,16,12,128]{4,2,3,1,0:T(8,128)} %copy-done.3) | copy-start | bytes 2949124
  91.4 1.8 %copy-start.14 = (f32[1,1,16,12,128]{4,2,3,1,0:T(8,128)S(1)}, f32[1,1,16,12,128]{4,2,3,1,0:T(8,128)}, u32[]{:S(2)}) copy-start(f32[1,1,16,12,128]{4,2,3,1,0:T(8,128)} %get-tuple-element.16) | copy-start | bytes 294916
  91.4 1.8 %copy-start.15 = (f32[1,1,16,12,128]{4,2,3,1,0:T(8,128)S(1)}, f32[1,1,16,12,128]{4,2,3,1,0:T(8,128)}, u32[]{:S(2)}) copy-start(f32[1,1,16,12,128]{4,2,3,1,0:T(8,128)} %get-tuple-element.23) | copy-start | bytes 294916
  94.4 0.9 copy-start.12
  94.4 0.9 copy-start.13
where the time goes:
time: 98.3 us; the launch traced here: 97.6 us
  waiting for transfers between devices  26.8 us (27%)
  starting transfers between devices  26.1 us (27%)
  matrix products  16.1 us (16%)
  other arithmetic  15.4 us (16%)
  local copies, waits for them, and re-layouts  12.7 us (13%)
    ppermute x1, waiting for transfers between devices, with_halo(): before = lax.ppermute(last, axis, up)  11.4 us
    dot_general x1, matrix products, theta_derivatives(): slope_t = jnp.dot(work_fields, theta_first, precision=highest)  8.68 us
    all_to_all x1, waiting for transfers between devices, per_device(): lax.all_to_all(curve_r, 'pen', split_axis=3, concat_axis=2, tiled=True)  8.63 us
    ppermute x1, starting transfers between devices, with_halo(): after = lax.ppermute(initial, axis, down)  6.88 us
    ppermute x1, waiting for transfers between devices, with_halo(): after = lax.ppermute(initial, axis, down)  6.69 us
    all_to_all x1, starting transfers between devices, per_device(): lax.all_to_all(slope_r, 'pen', split_axis=3, concat_axis=2, tiled=True)  6.24 us
    all_to_all x1, starting transfers between devices, per_device(): lax.all_to_all(curve_r, 'pen', split_axis=3, concat_axis=2, tiled=True)  5.85 us
    dot_general x1, matrix products, theta_derivatives(): jnp.dot(work_fields[:, :4], azimuthal_second_derivative, precision=highest)  5.32 us
  transfers between devices with their start and end apart: 5, of which 3 were waited for; matrix products, arithmetic and copies ran while one was open for 28% of the time, Pallas kernels for 0%

commit v1 on v0

--- a/solution.py
+++ b/solution.py
@@ -188,7 +188,12 @@
     )
     slope_r, curve_r = (
         lax.all_to_all(slope_r, "pen", split_axis=3, concat_axis=2, tiled=True),
-        lax.all_to_all(curve_r, "pen", split_axis=3, concat_axis=2, tiled=True),
+        jnp.concatenate(
+            lax.all_to_all(
+                jnp.stack(jnp.split(curve_r, lax.axis_size("pen"), axis=3)), "pen", 0, 0
+            ),
+            axis=2,
+        ),
     )
     radial_component = radial_terms(slope_r, curve_r, radial_mean, density, pressure, inv_local)
     return radial_component + other_terms(

time: 98.3 us -> 91.5 us (0.931)
  the two profiles are of different devices: /device:TPU:4 before, /device:TPU:1 now
where the time goes in v1:
time: 91.5 us; the launch traced here: 90.7 us
  starting transfers between devices  27.9 us (30%)
  waiting for transfers between devices  26.6 us (29%)
  other arithmetic  16.6 us (18%)
  local copies, waits for them, and re-layouts  12.7 us (14%)
  matrix products  6.39 us (7%)
    all_to_all x1, waiting for transfers between devices, per_device(): lax.all_to_all(slope_r, 'pen', split_axis=3, concat_axis=2, tiled=True)  13.9 us
    all_to_all x1, starting transfers between devices, per_device(): lax.all_to_all(work_fields, 'pen', split_axis=2, concat_axis=3, tiled=True)  10.4 us
    all_to_all x1, waiting for transfers between devices, per_device(): lax.all_to_all(jnp.stack(jnp.split(curve_r, lax.axis_size('pen'), axis=3)...  7.38 us
    ppermute x1, starting transfers between devices, with_halo(): before = lax.ppermute(last, axis, up)  6.83 us
    unnamed x7, other arithmetic  6 us
    all_to_all x1, waiting for transfers between devices, per_device(): lax.all_to_all(work_fields, 'pen', split_axis=2, concat_axis=3, tiled=True)  5.25 us
    all_to_all x1, starting transfers between devices, per_device(): lax.all_to_all(jnp.stack(jnp.split(curve_r, lax.axis_size('pen'), axis=3)...  4.98 us
    all_to_all x1, starting transfers between devices, per_device(): lax.all_to_all(slope_r, 'pen', split_axis=3, concat_axis=2, tiled=True)  4.45 us
  transfers between devices with their start and end apart: 5, of which 3 were waited for; matrix products, arithmetic and copies ran while one was open for 22% of the time, Pallas kernels for 0%

profile of v1, /device:TPU:1, one launch (start us, length us, event | category | flops | bytes accessed | tf_op | source)
XLA Modules:
  0.0 90.7 jit_solution(7710087340681799523)
XLA Ops:
  0.0 1.1 %slice.247 = f32[2,2,16,12,128]{4,2,3,1,0:T(8,128)S(1)} slice(f32[2,5,16,12,128]{4,2,3,1,0:T(8,128)} %param.11), slice={[0:2], [3:5], [0:16], [0:12], [0:128]} | slice | bytes 786432 | tf_op jit(solution)/shard_map/slice | solution.py:72
  1.1 1.1 %slice.244 = f32[2,3,16,12,128]{4,2,3,1,0:T(8,128)S(1)} slice(f32[2,5,16,12,128]{4,2,3,1,0:T(8,128)} %param.11), slice={[0:2], [0:3], [0:16], [0:12], [0:128]} | slice | bytes 1179648 | tf_op jit(solution)/shard_map/slice | solution.py:72
  2.3 0.0 copy-done.1
  2.3 0.0 copy-done
  2.3 0.0 copy-done.18
  2.3 0.1 divide_subtract_fusion
  2.4 0.1 pad_maximum_fusion.1
  2.5 0.9 %fusion.69 = (f32[2,6,4,12,128]{4,2,3,1,0:T(4,128)}, f32[2,6,4,12,128]{4,2,3,1,0:T(4,128)}) fusion(f32[2,6,16,12,128]{4,2,3,1,0:T(8,128)S(1)} %pad_maximum_fusion.1), kind=kLoop, calls=%fused_computation.140 | loop fusion | bytes 1179648 | tf_op jit(solution)/shard_map/slice | solution.py:25
  3.4 1.3 %collective-permute-start = (f32[2,6,4,12,128]{4,2,3,1,0:T(4,128)}, f32[2,6,4,12,128]{4,2,3,1,0:T(4,128)}, u32[]{:S(2)}, u32[]{:S(2)}) collective-permute-start(f32[2,6,4,12,128]{4,2,3,1,0:T(4,128)} %get-tuple-element.11), channel_id=1, source_target_pairs={{16,0},{32,16},{48,32},{64,48},{80,64},{96,80},{112,96},{128,112},... | collective-permute-start | bytes 884744 | tf_op jit(solution)/shard_map/ppermute | solution.py:27
  4.7 6.8 %collective-permute-start.1 = (f32[2,6,4,12,128]{4,2,3,1,0:T(4,128)}, f32[2,6,4,12,128]{4,2,3,1,0:T(4,128)}, u32[]{:S(2)}, u32[]{:S(2)}) collective-permute-start(f32[2,6,4,12,128]{4,2,3,1,0:T(4,128)} %get-tuple-element.12), channel_id=1, source_target_pairs={{0,16},{16,32},{32,48},{48,64},{64,80},{80,96},{96,112},{112,128},... | collective-permute-start | bytes 884744 | tf_op jit(solution)/shard_map/ppermute | solution.py:26
  11.5 1.9 %copy.108 = f32[2,6,16,12,128]{4,0,3,1,2:T(2,128)} copy(f32[2,6,16,12,128]{4,2,3,1,0:T(8,128)S(1)} %pad_maximum_fusion.1) | data formatting | bytes 2359296 | tf_op jit(solution)/shard_map/concatenate | solution.py:72
  13.4 10.4 %all-to-all-start = ((f32[2,6,16,12,128]{4,0,3,1,2:T(2,128)}), f32[2,6,16,12,128]{4,0,3,1,2:T(2,128)S(1)}, u32[]{:S(2)}, u32[]{:S(2)}) async-start(f32[2,6,16,12,128]{4,0,3,1,2:T(2,128)} %copy.108), calls=%async_computation | async-start | bytes 2359296 | tf_op jit(solution)/shard_map/all_to_all | solution.py:185
  23.8 0.0 copy-done.21
  23.8 0.1 broadcast_multiply_fusion.6
  23.9 1.6 %broadcast_multiply_fusion.2 = (f32[16,12,128]{2,0,1:T(8,128)}, f32[16,12,128]{2,0,1:T(8,128)S(1)}, f32[16,12,128]{2,0,1:T(8,128)S(1)}) fusion(f32[16,12,128]{2,0,1:T(8,128)S(1)} %copy-done.8, f32[12]{0:T(128)S(1)} %get-tuple-element.30, f32[12]{0:T(128)S(1)} %get-tuple-element.32, f32[16,12,128]{2,0,1:T(8,128)} %param.12), kind=kLoop, calls=%fused_computation.132 | loop fusion | flops 73728 | bytes 491616 | tf_op jit(solution)/shard_map/mul | solution.py:147
  25.5 0.9 broadcast_multiply_fusion.5
  26.4 1.0 %slice_multiply_fusion.10 = (f32[1,1,16,12,128]{4,2,3,1,0:T(8,128)}, f32[1,1,16,12,128]{4,2,3,1,0:T(8,128)}, f32[1,1,16,12,128]{4,2,3,1,0:T(8,128)}, f32[1,1,16,...) fusion(f32[2,5,16,12,128]{4,2,3,1,0:T(8,128)S(1)} %copy-done), kind=kLoop, calls=%fused_computation.91 | loop fusion | flops 245760 | bytes 1966080 | tf_op jit(solution)/shard_map/mul | solution.py:107
  27.4 0.0 collective-permute-done
  27.4 0.0 collective-permute-done.1
  27.4 1.5 %pad_maximum_fusion = (f32[2,6,20,12,128]{4,2,3,1,0:T(8,128)S(1)}, f32[2,6,20,12,128]{4,2,3,1,0:T(8,128)S(1)}) fusion(f32[2,6,4,12,128]{4,2,3,1,0:T(4,128)} %collective-permute-done, f32[2,2,16,12,128]{4,2,3,1,0:T(8,128)S(1)} %slice.247, f32[2,1,16,12,128]{4,2,3,1,0:T(8,128)S(1)} %divide_subtract_fusion, f32[2,3,16,12,128]{4,2,3,1,0:T(8,128)S(1)} %slice.244, ...), kind=kLoop, calls=%fused_computation | loop fusion | flops 2211840 | bytes 4718592 | tf_op jit(solution)/shard_map/concatenate | solution.py:28
  28.9 3.0 %multiply_add_fusion = (f32[2,6,16,12,128]{4,2,3,1,0:T(8,128)S(1)}, f32[2,6,16,12,128]{4,2,3,1,0:T(8,128)S(1)}, f32[2,6,16,12,128]{4,2,3,1,0:T(8,128)}) fusion(f32[16,12,128]{2,0,1:T(8,128)S(1)} %get-tuple-element.29, f32[16,12,128]{2,0,1:T(8,128)S(1)} %get-tuple-element.34, f32[2,6,20,12,128]{4,2,3,1,0:T(8,128)S(1)} %get-tuple-element.10, ...), kind=kOutput, calls=%fused_computation.19 | convolution fusion | flops 457703424 | bytes 14417920 | tf_op jit(solution)/shard_map/dot_general | solution.py:95
  31.8 0.1 broadcast_multiply_fusion
  31.9 0.8 copy-done.22
  32.7 1.4 %fusion = f32[2,4,16,12,128]{4,2,3,1,0:T(8,128)S(1)} fusion(f32[128,128,1,1,1]{1,0,4,3,2:T(8,128)S(1)} %copy-done.22, f32[2,6,20,12,128]{4,2,3,1,0:T(8,128)S(1)} %get-tuple-element.10, f32[2,6,20,12,128]{4,2,3,1,0:T(8,128)S(1)} %get-tuple-element.9, f32[2,1,16,12,128]{4,2,3,1,0:T(8,128)S(1)} %divide_subtract_fusion, f32[2,3,16,12,128]{4,2,3,1,0:T(8,128)S(1)} %slice.244, ...), kind=kOutput, calls=%fused_computation.5 | convolution fusion | flops 305528832 | bytes 8716800 | tf_op jit(solution)/shard_map/dot_general | solution.py:96
  34.1 0.9 copy-done.6
  35.0 0.7 fusion.38
  35.8 5.3 %all-to-all-done = f32[2,6,16,12,128]{4,0,3,1,2:T(2,128)S(1)} async-done(((f32[2,6,16,12,128]{4,0,3,1,2:T(2,128)}), f32[2,6,16,12,128]{4,0,3,1,2:T(2,128)S(1)}, u32[]{:S(2)}, u32[]{:S(2)}) %all-to-all-start) | async-done | bytes 1179680 | tf_op jit(solution)/shard_map/all_to_all | solution.py:185
  41.0 0.1 copy.109
  41.1 0.8 copy-done.20
  41.9 1.2 %convolution_bitcast_fusion = f32[2,6,1,192,128]{4,3,1,0,2:T(8,128)S(1)} fusion(f32[192,192,1,1]{1,0,3,2:T(8,128)S(1)} %copy-done.20, f32[2,6,192,128]{3,0,2,1:T(2,128)S(1)} %bitcast.102), kind=kOutput, calls=%fused_computation.2 | convolution fusion | flops 679477248 | bytes 2506752 | tf_op jit(solution)/shard_map/sj,abxjt->abxst/dot_general | solution.py:101
  43.1 1.9 %copy.111 = f32[2,6,1,192,128]{4,0,2,1,3:T(2,128)} copy(f32[2,6,1,192,128]{4,3,1,0,2:T(8,128)S(1)} %convolution_bitcast_fusion) | data formatting | bytes 2359296 | tf_op jit(solution)/shard_map/sj,abxjt->abxst/transpose | solution.py:101
  45.1 4.5 %all-to-all-start.1 = ((f32[2,6,1,192,128]{4,0,2,1,3:T(2,128)}), f32[2,6,1,192,128]{4,0,2,1,3:T(2,128)S(1)}, u32[]{:S(2)}, u32[]{:S(2)}) async-start(f32[2,6,1,192,128]{4,0,2,1,3:T(2,128)} %copy.111), calls=%async_computation.1 | async-start | bytes 2359296 | tf_op jit(solution)/shard_map/all_to_all | solution.py:190
  49.5 0.1 slice.306
  49.6 0.9 copy-done.19
  50.4 0.9 convolution_bitcast_fusion.1
  51.6 1.2 %copy.116 = f32[16,2,4,1,12,128]{5,2,4,3,1,0:T(4,128)} copy(f32[16,2,4,1,12,128]{5,4,2,1,3,0:T(8,128)S(1)} %fusion.50) | data formatting | bytes 1572864 | tf_op jit(solution)/shard_map/stack | solution.py:193
  52.8 13.9 %all-to-all-done.1 = f32[2,6,1,192,128]{4,0,2,1,3:T(2,128)S(1)} async-done(((f32[2,6,1,192,128]{4,0,2,1,3:T(2,128)}), f32[2,6,1,192,128]{4,0,2,1,3:T(2,128)S(1)}, u32[]{:S(2)}, u32[]{:S(2)}) %all-to-all-start.1) | async-done | bytes 1179680 | tf_op jit(solution)/shard_map/all_to_all | solution.py:190
  66.7 5.0 %all-to-all-start.2 = ((f32[16,2,4,1,12,128]{5,2,4,3,1,0:T(4,128)}), f32[16,2,4,1,12,128]{5,2,4,3,1,0:T(4,128)}, u32[]{:S(2)}, u32[]{:S(2)}) async-start(f32[16,2,4,1,12,128]{5,2,4,3,1,0:T(4,128)} %copy.116), calls=%async_computation.2 | async-start | bytes 1572864 | tf_op jit(solution)/shard_map/all_to_all | solution.py:192
  71.7 2.0 %fusion.35 = f32[2,5,16,12,128]{4,2,3,1,0:T(8,128)} fusion(f32[2,5,16,12,128]{4,2,3,1,0:T(8,128)} %fusion.38, f32[2,4,16,12,128]{4,2,3,1,0:T(8,128)S(1)} %copy-done.7, f32[2,6,16,12,128]{4,2,3,1,0:T(8,128)} %copy-done.5, f32[1,1,16,12,128]{4,2,3,1,0:T(8,128)} %get-tuple-element.19, f32[1,1,16,12,128]{4,2,3,1,0:T(8,128)} %get-tuple-element.20, ...), kind=kLoop, calls=%fused_computation.63 | loop fusion | flops 491520 | bytes 1474608
  73.7 2.0 %fusion.29 = f32[2,5,16,12,128]{4,2,3,1,0:T(8,128)} fusion(f32[2,5,16,12,128]{4,2,3,1,0:T(8,128)} %fusion.35, f32[2,6,16,12,128]{4,2,3,1,0:T(8,128)} %get-tuple-element.33, f32[2,4,16,12,128]{4,2,3,1,0:T(8,128)S(1)} %copy-done.7, f32[2,6,16,12,128]{4,2,3,1,0:T(8,128)} %copy-done.5, f32[1,1,16,12,128]{4,2,3,1,0:T(8,128)S(1)} %copy-done.16, ...), kind=kLoop, calls=%fused_computation.54 | loop fusion | flops 786432 | bytes 1867872
  75.7 1.4 %broadcast_multiply_fusion.1 = (f32[2,6,16,12,128]{4,2,3,1,0:T(8,128)}, f32[2,6,16,12,128]{4,2,3,1,0:T(8,128)S(1)}) fusion(f32[16,12,128]{2,0,1:T(8,128)S(1)} %copy-done.11, f32[2,6,16,12,128]{4,0,1,3,2:T(2,128)S(1)} %bitcast.104), kind=kLoop, calls=%fused_computation.38 | loop fusion | flops 294912 | bytes 3637248 | tf_op jit(solution)/shard_map/mul | solution.py:112
  77.1 7.4 %all-to-all-done.2 = f32[16,2,4,1,12,128]{5,2,4,3,1,0:T(4,128)} async-done(((f32[16,2,4,1,12,128]{5,2,4,3,1,0:T(4,128)}), f32[16,2,4,1,12,128]{5,2,4,3,1,0:T(4,128)}, u32[]{:S(2)}, u32[]{:S(2)}) %all-to-all-start.2) | async-done | bytes 786464 | tf_op jit(solution)/shard_map/all_to_all | solution.py:192
  84.5 1.8 %fusion.18 = f32[2,4,16,12,128]{4,2,3,1,0:T(8,128)S(1)} fusion(f32[2,6,16,12,128]{4,2,3,1,0:T(8,128)S(1)} %get-tuple-element.14, f32[16,2,4,1,12,128]{5,2,4,3,1,0:T(4,128)} %all-to-all-done.2, f32[12]{0:T(128)S(1)} %get-tuple-element.32), kind=kLoop, calls=%fused_computation.34 | loop fusion | flops 393216 | bytes 2359344 | tf_op jit(solution)/shard_map/add | solution.py:111
  86.3 1.2 %fusion.23 = (f32[2,5,16,12,128]{4,2,3,1,0:T(8,128)S(1)}, f32[2,1,16,12,128]{4,2,3,1,0:T(8,128)S(1)}, f32[2,5,16,12,128]{4,2,3,1,0:T(8,128)S(1)}) fusion(f32[2,5,16,12,128]{4,2,3,1,0:T(8,128)S(1)} %copy-done.4, f32[2,6,16,12,128]{4,2,3,1,0:T(8,128)} %copy-done.5, f32[1,1,16,12,128]{4,2,3,1,0:T(8,128)S(1)} %copy-done.15, ...), kind=kLoop, calls=%fused_computation.47 | loop fusion | flops 540672 | bytes 2261504
  87.6 0.8 copy-done.12
  88.4 0.0 copy-done.13
  88.5 1.1 %fusion.20 = (f32[2,5,16,12,128]{4,2,3,1,0:T(8,128)S(1)}, f32[2,5,16,12,128]{4,2,3,1,0:T(8,128)S(1)}) fusion(f32[2,5,16,12,128]{4,2,3,1,0:T(8,128)S(1)} %get-tuple-element.5, f32[2,4,16,12,128]{4,2,3,1,0:T(8,128)} %copy-done.6, f32[2,6,16,12,128]{4,2,3,1,0:T(8,128)} %copy-done.5, f32[1,1,16,12,128]{4,2,3,1,0:T(8,128)S(1)} %copy-done.13, ...), kind=kLoop, calls=%fused_computation.41 | loop fusion | flops 491520 | bytes 1867776 | tf_op jit(solution)/shard_map/stack | solution.py:164
  89.6 1.1 %add.150 = f32[2,5,16,12,128]{4,2,3,1,0:T(8,128)} add(f32[2,5,16,12,128]{4,2,3,1,0:T(8,128)S(1)} %get-tuple-element.26, f32[2,5,16,12,128]{4,2,3,1,0:T(8,128)S(1)} %get-tuple-element.25) | non-fusion elementwise | flops 245760 | bytes 2949120 | tf_op jit(solution)/shard_map/add | solution.py:199
  (58 shorter events, 0.3 us)
Async XLA Ops:
  0.0 2.3 %copy-start = (f32[2,5,16,12,128]{4,2,3,1,0:T(8,128)S(1)}, f32[2,5,16,12,128]{4,2,3,1,0:T(8,128)}, u32[]{:S(2)}) copy-start(f32[2,5,16,12,128]{4,2,3,1,0:T(8,128)} %param.11) | copy-start | bytes 2949124
  0.0 2.3 %copy-start.1 = (f32[16,12,128]{2,0,1:T(8,128)S(1)}, f32[16,12,128]{2,0,1:T(8,128)}, u32[]{:S(2)}) copy-start(f32[16,12,128]{2,0,1:T(8,128)} %param.15) | copy-start | bytes 294916
  0.0 2.3 %copy-start.18 = (f32[16,12,128]{2,0,1:T(8,128)S(1)}, f32[16,12,128]{2,0,1:T(8,128)}, u32[]{:S(2)}) copy-start(f32[16,12,128]{2,0,1:T(8,128)} %param.16) | copy-start | bytes 294916
  3.4 24.0 %collective-permute-start = (f32[2,6,4,12,128]{4,2,3,1,0:T(4,128)}, f32[2,6,4,12,128]{4,2,3,1,0:T(4,128)}, u32[]{:S(2)}, u32[]{:S(2)}) collective-permute-start(f32[2,6,4,12,128]{4,2,3,1,0:T(4,128)} %get-tuple-element.11), channel_id=1, source_target_pairs={{16,0},{32,16},{48,32},{64,48},{80,64},{96,80},{112,96},{128,112},... | collective-permute-start | bytes 884744 | tf_op jit(solution)/shard_map/ppermute | solution.py:27
  4.7 22.7 %collective-permute-start.1 = (f32[2,6,4,12,128]{4,2,3,1,0:T(4,128)}, f32[2,6,4,12,128]{4,2,3,1,0:T(4,128)}, u32[]{:S(2)}, u32[]{:S(2)}) collective-permute-start(f32[2,6,4,12,128]{4,2,3,1,0:T(4,128)} %get-tuple-element.12), channel_id=1, source_target_pairs={{0,16},{16,32},{32,48},{48,64},{64,80},{80,96},{96,112},{112,128},... | collective-permute-start | bytes 884744 | tf_op jit(solution)/shard_map/ppermute | solution.py:26
  13.4 10.4 %copy-start.21 = (f32[192]{0:T(256)S(1)}, f32[192]{0:T(256)}, u32[]{:S(2)}) copy-start(f32[192]{0:T(256)} %constant.58.clone) | copy-start | bytes 2308
  13.4 10.5 %copy-start.8 = (f32[16,12,128]{2,0,1:T(8,128)S(1)}, f32[16,12,128]{2,0,1:T(8,128)}, u32[]{:S(2)}) copy-start(f32[16,12,128]{2,0,1:T(8,128)} %param.14) | copy-start | bytes 294916
  13.4 27.6 %all-to-all-start = ((f32[2,6,16,12,128]{4,0,3,1,2:T(2,128)}), f32[2,6,16,12,128]{4,0,3,1,2:T(2,128)S(1)}, u32[]{:S(2)}, u32[]{:S(2)}) async-start(f32[2,6,16,12,128]{4,0,3,1,2:T(2,128)} %copy.108), calls=%async_computation | async-start | bytes 2359296 | tf_op jit(solution)/shard_map/all_to_all | solution.py:185
  27.4 1.5 %copy-start.23 = (f32[128,128,1,1,1]{1,0,4,3,2:T(8,128)S(1)}, f32[128,128,1,1,1]{1,0,4,3,2:T(8,128)}, u32[]{:S(2)}) copy-start(f32[128,128,1,1,1]{1,0,4,3,2:T(8,128)} %constant.69) | copy-start | bytes 196612
  31.8 2.3 %copy-start.5 = (f32[2,6,16,12,128]{4,2,3,1,0:T(8,128)}, f32[2,6,16,12,128]{4,2,3,1,0:T(8,128)S(1)}, u32[]{:S(2)}) copy-start(f32[2,6,16,12,128]{4,2,3,1,0:T(8,128)S(1)} %get-tuple-element.7) | copy-start | bytes 3538948
  31.8 0.9 copy-start.22
  31.9 2.2 %copy-start.3 = (f32[2,6,16,12,128]{4,2,3,1,0:T(8,128)}, f32[2,6,16,12,128]{4,2,3,1,0:T(8,128)S(1)}, u32[]{:S(2)}) copy-start(f32[2,6,16,12,128]{4,2,3,1,0:T(8,128)S(1)} %broadcast_multiply_fusion) | copy-start | bytes 3538948
  34.1 0.9 %copy-start.6 = (f32[2,4,16,12,128]{4,2,3,1,0:T(8,128)}, f32[2,4,16,12,128]{4,2,3,1,0:T(8,128)S(1)}, u32[]{:S(2)}) copy-start(f32[2,4,16,12,128]{4,2,3,1,0:T(8,128)S(1)} %fusion) | copy-start | bytes 2359300
  41.0 0.9 %copy-start.20 = (f32[192,192,1,1]{1,0,3,2:T(8,128)S(1)}, f32[192,192,1,1]{1,0,3,2:T(8,128)}, u32[]{:S(2)}) copy-start(f32[192,192,1,1]{1,0,3,2:T(8,128)} %constant.67) | copy-start | bytes 442372
  45.1 21.7 %all-to-all-start.1 = ((f32[2,6,1,192,128]{4,0,2,1,3:T(2,128)}), f32[2,6,1,192,128]{4,0,2,1,3:T(2,128)S(1)}, u32[]{:S(2)}, u32[]{:S(2)}) async-start(f32[2,6,1,192,128]{4,0,2,1,3:T(2,128)} %copy.111), calls=%async_computation.1 | async-start | bytes 2359296 | tf_op jit(solution)/shard_map/all_to_all | solution.py:190
  49.5 0.9 %copy-start.19 = (f32[192,192,1,1]{1,0,3,2:T(8,128)S(1)}, f32[192,192,1,1]{1,0,3,2:T(8,128)}, u32[]{:S(2)}) copy-start(f32[192,192,1,1]{1,0,3,2:T(8,128)} %constant.68) | copy-start | bytes 442372
  52.8 18.9 %copy-start.7 = (f32[2,4,16,12,128]{4,2,3,1,0:T(8,128)S(1)}, f32[2,4,16,12,128]{4,2,3,1,0:T(8,128)}, u32[]{:S(2)}) copy-start(f32[2,4,16,12,128]{4,2,3,1,0:T(8,128)} %copy-done.6) | copy-start | bytes 2359300
  52.8 20.9 %copy-start.9 = (f32[16,12,128]{2,0,1:T(8,128)S(1)}, f32[16,12,128]{2,0,1:T(8,128)}, u32[]{:S(2)}) copy-start(f32[16,12,128]{2,0,1:T(8,128)} %param.14) | copy-start | bytes 294916
  52.8 20.9 %copy-start.10 = (f32[16,12,128]{2,0,1:T(8,128)S(1)}, f32[16,12,128]{2,0,1:T(8,128)}, u32[]{:S(2)}) copy-start(f32[16,12,128]{2,0,1:T(8,128)} %param.13) | copy-start | bytes 294916
  52.8 20.9 %copy-start.16 = (f32[1,1,16,12,128]{4,2,3,1,0:T(8,128)S(1)}, f32[1,1,16,12,128]{4,2,3,1,0:T(8,128)}, u32[]{:S(2)}) copy-start(f32[1,1,16,12,128]{4,2,3,1,0:T(8,128)} %get-tuple-element.17) | copy-start | bytes 294916
  52.8 20.9 %copy-start.17 = (f32[1,1,16,12,128]{4,2,3,1,0:T(8,128)S(1)}, f32[1,1,16,12,128]{4,2,3,1,0:T(8,128)}, u32[]{:S(2)}) copy-start(f32[1,1,16,12,128]{4,2,3,1,0:T(8,128)} %get-tuple-element.18) | copy-start | bytes 294916
  66.7 17.7 %all-to-all-start.2 = ((f32[16,2,4,1,12,128]{5,2,4,3,1,0:T(4,128)}), f32[16,2,4,1,12,128]{5,2,4,3,1,0:T(4,128)}, u32[]{:S(2)}, u32[]{:S(2)}) async-start(f32[16,2,4,1,12,128]{5,2,4,3,1,0:T(4,128)} %copy.116), calls=%async_computation.2 | async-start | bytes 1572864 | tf_op jit(solution)/shard_map/all_to_all | solution.py:192
  73.7 2.0 %copy-start.11 = (f32[16,12,128]{2,0,1:T(8,128)S(1)}, f32[16,12,128]{2,0,1:T(8,128)}, u32[]{:S(2)}) copy-start(f32[16,12,128]{2,0,1:T(8,128)} %param.13) | copy-start | bytes 294916
  84.5 1.8 %copy-start.2 = (f32[2,6,16,12,128]{4,2,3,1,0:T(8,128)S(1)}, f32[2,6,16,12,128]{4,2,3,1,0:T(8,128)}, u32[]{:S(2)}) copy-start(f32[2,6,16,12,128]{4,2,3,1,0:T(8,128)} %get-tuple-element.13) | copy-start | bytes 3538948
  84.5 1.8 %copy-start.4 = (f32[2,5,16,12,128]{4,2,3,1,0:T(8,128)S(1)}, f32[2,5,16,12,128]{4,2,3,1,0:T(8,128)}, u32[]{:S(2)}) copy-start(f32[2,5,16,12,128]{4,2,3,1,0:T(8,128)} %fusion.29) | copy-start | bytes 2949124
  84.5 1.8 %copy-start.14 = (f32[1,1,16,12,128]{4,2,3,1,0:T(8,128)S(1)}, f32[1,1,16,12,128]{4,2,3,1,0:T(8,128)}, u32[]{:S(2)}) copy-start(f32[1,1,16,12,128]{4,2,3,1,0:T(8,128)} %get-tuple-element.16) | copy-start | bytes 294916
  84.5 1.8 %copy-start.15 = (f32[1,1,16,12,128]{4,2,3,1,0:T(8,128)S(1)}, f32[1,1,16,12,128]{4,2,3,1,0:T(8,128)}, u32[]{:S(2)}) copy-start(f32[1,1,16,12,128]{4,2,3,1,0:T(8,128)} %get-tuple-element.23) | copy-start | bytes 294916
  87.5 0.9 copy-start.12
  87.6 0.9 %copy-start.13 = (f32[1,1,16,12,128]{4,2,3,1,0:T(8,128)S(1)}, f32[1,1,16,12,128]{4,2,3,1,0:T(8,128)}, u32[]{:S(2)}) copy-start(f32[1,1,16,12,128]{4,2,3,1,0:T(8,128)} %get-tuple-element.24) | copy-start | bytes 294916
